TPU v7x, 512 devices: a whole 4x4x16 slice. The times are simulated.
512 devices in a mesh: adapter: 64 (over y, z), mp: 8 (over x, core).
Axes of the slice: x: 4, y: 4, z: 16, core: 2. Of those that a mesh axis runs over, the one named last changes fastest.
Arguments:
- tokens: bfloat16 [24576, 8192], P('adapter', 'mp'), may hold values from -6 to 6
- cotangent: bfloat16 [24576, 1024], P('adapter', 'mp'), may hold values from -6 to 6
- value_weight: bfloat16 [8192, 1024], P('mp', 'adapter'), may hold values from -0.0625 to 0.0625
- down_store: bfloat16 [128, 8, 1024, 64], P(None, 'mp', 'adapter'), may hold values from -0.0625 to 0.0625
- down_first: float32 [128, 8, 1024, 64], P(None, 'mp', 'adapter'), may hold values from -4 to 4
- down_second: float32 [128, 8, 1024, 64], P(None, 'mp', 'adapter'), may hold values from 0.01 to 1
- up_store: bfloat16 [128, 64, 1024], P(None, 'adapter', 'mp'), may hold values from -0.75 to 0.75
- up_first: float32 [128, 64, 1024], P(None, 'adapter', 'mp'), may hold values from -4 to 4
- up_second: float32 [128, 64, 1024], P(None, 'adapter', 'mp'), may hold values from 0.01 to 1
- tile_adapter: int32 [192], replicated, may hold values from 0 to 127
- tile_length: int32 [192], replicated, may hold values from 1 to 128, as said below
- adapter_slot: int32 [128], replicated, may hold values from 0 to 127, each once
Outputs:
- projected: bfloat16 [24576, 1024], P('adapter', 'mp')
- token_gradient: bfloat16 [24576, 8192], P('adapter', 'mp')
- new_down: float32 [128, 8, 1024, 64], P(None, 'mp', 'adapter')
- new_down_first: float32 [128, 8, 1024, 64], P(None, 'mp', 'adapter')
- new_down_second: float32 [128, 8, 1024, 64], P(None, 'mp', 'adapter')
- new_up: float32 [128, 64, 1024], P(None, 'adapter', 'mp')
- new_up_first: float32 [128, 64, 1024], P(None, 'adapter', 'mp')
- new_up_second: float32 [128, 64, 1024], P(None, 'adapter', 'mp')
Inputs may be any that keep to these rules, and one draw needn't show every extreme that they name: `tile_length`: some tile is full in every draw. `adapter_slot`: each slot holds exactly one adapter.
All inputs are finite; a program needn't handle non-finite values.
Results may differ from a plain program's by a relative error of at most 0.0046.
Values may be sent and summed in bfloat16 or wider, within the bound.
No kernel may reach another device: no remote copies, remote signals or barrier semaphores. Data moves between devices by JAX's collectives and lax.ppermute only.
A program may use at most 64 MiB of HBM per device.

v0:
```python
import jax
import jax.numpy as jnp
from jax import lax
from jax.sharding import Mesh, PartitionSpec as P

TILE = 128
STEP = 100
adapter_scale = 2.0
learn_rate = 0.001
beta_one = 0.9
beta_two = 0.999
adam_eps = 1e-08


def adam_step(store, first, second, gradient):
    new_first = beta_one * first + (1.0 - beta_one) * gradient
    new_second = beta_two * second + (1.0 - beta_two) * gradient * gradient
    corr_one = 1.0 - beta_one**STEP
    corr_two = 1.0 - beta_two**STEP
    moved = store.astype(jnp.float32) - learn_rate * (new_first / corr_one) / (
        jnp.sqrt(new_second / corr_two) + adam_eps
    )
    return (moved, new_first, new_second)


ADAPTER = ("ay", "az")


def gather_along(piece, axis):
    count = lax.axis_size(axis)
    got = [piece]
    for shift in range(1, count):
        pairs = [(j, (j - shift) % count) for j in range(count)]
        got.append(lax.ppermute(piece, axis, pairs))
    ordered = jnp.roll(jnp.stack(got), lax.axis_index(axis), axis=0)
    return jnp.moveaxis(ordered, 0, 1).reshape(piece.shape[0], count * piece.shape[1])


def gather_weight(value_weight):
    return gather_along(gather_along(value_weight, "az"), "ay")


def split_adapter(mesh):
    devices = mesh.devices
    n_adapter = devices.shape[0]
    try:
        n_y = len({d.coords[1] for d in devices[:, 0]})
    except (AttributeError, IndexError, TypeError):
        n_y = 1
    if n_y < 1 or n_adapter % n_y:
        n_y = 1
    return Mesh(devices.reshape(n_y, n_adapter // n_y, devices.shape[1]), ("ay", "az", "mp"))


def shards(
    tokens,
    cotangent,
    value_weight,
    down_store,
    down_first,
    down_second,
    up_store,
    up_first,
    up_second,
    tile_adapter,
    tile_length,
    adapter_slot,
):
    tile_total = tile_adapter.shape[0]
    tok_count, feat_part = tokens.shape
    head_cols = cotangent.shape[1]
    tiles_here = tok_count // TILE
    adapter_count = adapter_slot.shape[0]
    my_index = lax.axis_index(ADAPTER)
    adapter_ids = jnp.arange(adapter_count, dtype=jnp.int32)
    tile_adapter_slot = jnp.sum(
        jnp.where(tile_adapter[:, None] == adapter_ids[None, :], adapter_slot[None, :], 0), axis=1
    )
    my_lengths = lax.dynamic_slice_in_dim(tile_length, my_index * tiles_here, tiles_here)
    active_rows = (jnp.arange(TILE)[None, :] < my_lengths[:, None]).reshape(tok_count, 1)
    masked_own = cotangent * active_rows.astype(jnp.bfloat16)
    masked_full = lax.all_gather(masked_own, "mp", axis=1, tiled=True)
    n_adapter = tile_total // tiles_here
    row_part = down_store.shape[2]
    rank = down_store.shape[3]
    sent_down = down_store[:, 0][tile_adapter_slot].reshape(tile_total, row_part * rank)
    sent_up = up_store[tile_adapter_slot].reshape(tile_total, head_cols)
    sent = jnp.concatenate([sent_down, sent_up], axis=1)
    arrived = lax.all_to_all(sent, ADAPTER, split_axis=0, concat_axis=0, tiled=True)
    arrived = arrived.reshape(n_adapter, tiles_here, row_part * rank + head_cols)
    down_panel = (
        arrived[:, :, : row_part * rank]
        .reshape(n_adapter, tiles_here, row_part, rank)
        .transpose(1, 0, 2, 3)
        .reshape(tiles_here, n_adapter * row_part, rank)
    )
    up_panel = arrived[:, :, row_part * rank :].transpose(1, 0, 2)
    w_full = gather_weight(value_weight)
    token_tiles = tokens.reshape(tiles_here, TILE, feat_part)
    frozen_part = jnp.dot(tokens, w_full, preferred_element_type=jnp.float32)
    frozen_local = lax.psum_scatter(frozen_part, "mp", scatter_dimension=1, tiled=True)
    down_part = jnp.einsum(
        "ntd,ndr->ntr", token_tiles, down_panel, preferred_element_type=jnp.float32
    )
    down_sum = lax.psum(down_part, "mp")
    down_portion = down_sum.astype(jnp.bfloat16)
    adapter_term = jnp.einsum(
        "ntr,nrv->ntv", down_portion, up_panel, preferred_element_type=jnp.float32
    ).reshape(tok_count, head_cols)
    projected = (
        (frozen_local + adapter_scale * adapter_term) * active_rows.astype(jnp.float32)
    ).astype(jnp.bfloat16)
    tile_mask = masked_own.reshape(tiles_here, TILE, head_cols)
    backward_piece = adapter_scale * jnp.einsum(
        "ntv,nrv->ntr", tile_mask, up_panel, preferred_element_type=jnp.float32
    )
    backward_portion = lax.psum(backward_piece, "mp").astype(jnp.bfloat16)
    frozen_backward = lax.dot_general(
        masked_full, w_full, (((1,), (1,)), ((), ())), preferred_element_type=jnp.float32
    )
    adapter_backward = jnp.einsum(
        "ntr,ndr->ntd", backward_portion, down_panel, preferred_element_type=jnp.float32
    ).reshape(tok_count, feat_part)
    token_gradient = (frozen_backward + adapter_backward).astype(jnp.bfloat16)
    home_down = jnp.einsum(
        "ntd,ntr->ndr", token_tiles, backward_portion, preferred_element_type=jnp.float32
    )
    local_up_weight = adapter_scale * jnp.einsum(
        "ntr,ntv->nrv", down_portion, tile_mask, preferred_element_type=jnp.float32
    )
    grads = jnp.concatenate(
        [home_down.reshape(tiles_here, n_adapter, row_part * rank), local_up_weight], axis=2
    )
    grads = lax.all_to_all(grads, ADAPTER, split_axis=1, concat_axis=0, tiled=True)
    arrived_down = grads[:, 0, : row_part * rank]
    arrived_up = grads[:, 0, row_part * rank :]
    selector = (adapter_ids[:, None] == tile_adapter_slot[None, :]).astype(jnp.float32)
    down_gradient = jnp.dot(
        selector, arrived_down.reshape(tile_total, -1), precision=lax.Precision.HIGHEST
    ).reshape(down_store.shape)
    up_gradient = jnp.dot(
        selector, arrived_up.reshape(tile_total, -1), precision=lax.Precision.HIGHEST
    ).reshape(up_store.shape)
    new_down, new_down_first, new_down_second = adam_step(
        down_store, down_first, down_second, down_gradient
    )
    new_up, new_up_first, new_up_second = adam_step(up_store, up_first, up_second, up_gradient)
    return (
        projected,
        token_gradient,
        new_down,
        new_down_first,
        new_down_second,
        new_up,
        new_up_first,
        new_up_second,
    )


def solution(mesh):
    mesh = split_adapter(mesh)
    placed = (
        P(ADAPTER, "mp"),
        P(ADAPTER, "mp"),
        P("mp", ADAPTER),
        P(None, "mp", ADAPTER, None),
        P(None, "mp", ADAPTER, None),
        P(None, "mp", ADAPTER, None),
        P(None, ADAPTER, "mp"),
        P(None, ADAPTER, "mp"),
        P(None, ADAPTER, "mp"),
        P(),
        P(),
        P(),
    )
    return jax.shard_map(
        shards,
        mesh=mesh,
        in_specs=placed,
        out_specs=(
            P(ADAPTER, "mp"),
            P(ADAPTER, "mp"),
            P(None, "mp", ADAPTER, None),
            P(None, "mp", ADAPTER, None),
            P(None, "mp", ADAPTER, None),
            P(None, ADAPTER, "mp"),
            P(None, ADAPTER, "mp"),
            P(None, ADAPTER, "mp"),
        ),
        check_vma=False,
    )
```

profile of v0, /device:TPU:6, one launch (start us, length us, event | category | flops | bytes accessed | tf_op | source)
XLA Modules:
  0.0 261.7 jit_solution(3475305058610863027)
XLA Ops:
  7.2 11.5 %collective-permute-start = (bf16[1024,16]{0,1:T(8,128)(2,1)}, bf16[1024,16]{0,1:T(8,128)(2,1)S(1)}, u32[]{:S(2)}, u32[]{:S(2)}) collective-permute-start(bf16[1024,16]{0,1:T(8,128)(2,1)} %param.14), channel_id=1, source_target_pairs={{0,120},{8,0},{16,8},{24,16},{32,24},{40,32},{48,40},{56,48},{64,5... | collective-permute-start | bytes 98312 | tf_op jit(solution)/shard_map/ppermute | solution.py:34
  18.7 3.4 %collective-permute-start.1 = (bf16[1024,16]{0,1:T(8,128)(2,1)}, bf16[1024,16]{0,1:T(8,128)(2,1)S(1)}, u32[]{:S(2)}, u32[]{:S(2)}) collective-permute-start(bf16[1024,16]{0,1:T(8,128)(2,1)} %param.14), channel_id=1, source_target_pairs={{0,112},{8,120},{16,0},{24,8},{32,16},{40,24},{48,32},{56,40},{64,... | collective-permute-start | bytes 98312 | tf_op jit(solution)/shard_map/ppermute | solution.py:34
  22.1 5.0 %collective-permute-start.2 = (bf16[1024,16]{0,1:T(8,128)(2,1)}, bf16[1024,16]{0,1:T(8,128)(2,1)S(1)}, u32[]{:S(2)}, u32[]{:S(2)}) collective-permute-start(bf16[1024,16]{0,1:T(8,128)(2,1)} %param.14), channel_id=1, source_target_pairs={{0,104},{8,112},{16,120},{24,0},{32,8},{40,16},{48,24},{56,32},{64... | collective-permute-start | bytes 98312 | tf_op jit(solution)/shard_map/ppermute | solution.py:34
  27.1 2.8 %collective-permute-start.3 = (bf16[1024,16]{0,1:T(8,128)(2,1)}, bf16[1024,16]{0,1:T(8,128)(2,1)S(1)}, u32[]{:S(2)}, u32[]{:S(2)}) collective-permute-start(bf16[1024,16]{0,1:T(8,128)(2,1)} %param.14), channel_id=1, source_target_pairs={{0,96},{8,104},{16,112},{24,120},{32,0},{40,8},{48,16},{56,24},{64... | collective-permute-start | bytes 98312 | tf_op jit(solution)/shard_map/ppermute | solution.py:34
  30.0 1.9 collective-permute-start.4
  31.9 0.9 select_reduce_fusion
  32.8 1.4 copy.76
  34.2 0.8 gather_fusion
  35.0 0.5 concatenate.23
  35.5 1.5 gather_fusion.1
  37.0 1.1 pad_maximum_fusion.1
  38.1 15.8 %all-to-all-start = ((bf16[64,3,1152]{2,1,0:T(4,128)(2,1)}), bf16[64,3,1152]{2,1,0:T(4,128)(2,1)S(1)}, u32[]{:S(2)}, u32[]{:S(2)}) async-start(bf16[64,3,1152]{2,1,0:T(4,128)(2,1)} %pad_maximum_fusion.1), calls=%async_computation.1 | async-start | bytes 1179648 | tf_op jit(solution)/shard_map/all_to_all | solution.py:89
  53.9 0.1 dynamic_slice.13
  54.0 10.4 %collective-permute-start.5 = (bf16[1024,16]{0,1:T(8,128)(2,1)S(1)}, bf16[1024,16]{0,1:T(8,128)(2,1)S(1)}, u32[]{:S(2)}, u32[]{:S(2)}) collective-permute-start(bf16[1024,16]{0,1:T(8,128)(2,1)S(1)} %copy-done.3), channel_id=1, source_target_pairs={{0,80},{8,88},{16,96},{24,104},{32,112},{40,120},{48,0},{56,8},{64... | collective-permute-start | bytes 98312 | tf_op jit(solution)/shard_map/ppermute | solution.py:34
  64.4 4.3 %collective-permute-start.6 = (bf16[1024,16]{0,1:T(8,128)(2,1)S(1)}, bf16[1024,16]{0,1:T(8,128)(2,1)S(1)}, u32[]{:S(2)}, u32[]{:S(2)}) collective-permute-start(bf16[1024,16]{0,1:T(8,128)(2,1)S(1)} %copy-done.3), channel_id=1, source_target_pairs={{0,72},{8,80},{16,88},{24,96},{32,104},{40,112},{48,120},{56,0},{6... | collective-permute-start | bytes 98312 | tf_op jit(solution)/shard_map/ppermute | solution.py:34
  68.7 9.4 %collective-permute-start.7 = (bf16[1024,16]{0,1:T(8,128)(2,1)S(1)}, bf16[1024,16]{0,1:T(8,128)(2,1)S(1)}, u32[]{:S(2)}, u32[]{:S(2)}) collective-permute-start(bf16[1024,16]{0,1:T(8,128)(2,1)S(1)} %copy-done.3), channel_id=1, source_target_pairs={{0,64},{8,72},{16,80},{24,88},{32,96},{40,104},{48,112},{56,120},{... | collective-permute-start | bytes 98312 | tf_op jit(solution)/shard_map/ppermute | solution.py:34
  78.1 3.1 %collective-permute-start.8 = (bf16[1024,16]{0,1:T(8,128)(2,1)S(1)}, bf16[1024,16]{0,1:T(8,128)(2,1)S(1)}, u32[]{:S(2)}, u32[]{:S(2)}) collective-permute-start(bf16[1024,16]{0,1:T(8,128)(2,1)S(1)} %copy-done.3), channel_id=1, source_target_pairs={{0,56},{8,64},{16,72},{24,80},{32,88},{40,96},{48,104},{56,112},{6... | collective-permute-start | bytes 98312 | tf_op jit(solution)/shard_map/ppermute | solution.py:34
  81.2 10.3 %collective-permute-start.9 = (bf16[1024,16]{0,1:T(8,128)(2,1)S(1)}, bf16[1024,16]{0,1:T(8,128)(2,1)S(1)}, u32[]{:S(2)}, u32[]{:S(2)}) collective-permute-start(bf16[1024,16]{0,1:T(8,128)(2,1)S(1)} %copy-done.3), channel_id=1, source_target_pairs={{0,48},{8,56},{16,64},{24,72},{32,80},{40,88},{48,96},{56,104},{64... | collective-permute-start | bytes 98312 | tf_op jit(solution)/shard_map/ppermute | solution.py:34
  91.5 6.7 %collective-permute-start.10 = (bf16[1024,16]{0,1:T(8,128)(2,1)S(1)}, bf16[1024,16]{0,1:T(8,128)(2,1)S(1)}, u32[]{:S(2)}, u32[]{:S(2)}) collective-permute-start(bf16[1024,16]{0,1:T(8,128)(2,1)S(1)} %copy-done.3), channel_id=1, source_target_pairs={{0,40},{8,48},{16,56},{24,64},{32,72},{40,80},{48,88},{56,96},{64,... | collective-permute-start | bytes 98312 | tf_op jit(solution)/shard_map/ppermute | solution.py:34
  98.2 1.9 collective-permute-start.11
  100.2 5.2 %collective-permute-start.12 = (bf16[1024,16]{0,1:T(8,128)(2,1)S(1)}, bf16[1024,16]{0,1:T(8,128)(2,1)S(1)}, u32[]{:S(2)}, u32[]{:S(2)}) collective-permute-start(bf16[1024,16]{0,1:T(8,128)(2,1)S(1)} %copy-done.3), channel_id=1, source_target_pairs={{0,24},{8,32},{16,40},{24,48},{32,56},{40,64},{48,72},{56,80},{64,... | collective-permute-start | bytes 98312 | tf_op jit(solution)/shard_map/ppermute | solution.py:34
  105.5 2.7 %collective-permute-start.13 = (bf16[1024,16]{0,1:T(8,128)(2,1)S(1)}, bf16[1024,16]{0,1:T(8,128)(2,1)S(1)}, u32[]{:S(2)}, u32[]{:S(2)}) collective-permute-start(bf16[1024,16]{0,1:T(8,128)(2,1)S(1)} %copy-done.3), channel_id=1, source_target_pairs={{0,16},{8,24},{16,32},{24,40},{32,48},{40,56},{48,64},{56,72},{64,... | collective-permute-start | bytes 98312 | tf_op jit(solution)/shard_map/ppermute | solution.py:34
  108.1 4.8 %collective-permute-start.14 = (bf16[1024,16]{0,1:T(8,128)(2,1)S(1)}, bf16[1024,16]{0,1:T(8,128)(2,1)S(1)}, u32[]{:S(2)}, u32[]{:S(2)}) collective-permute-start(bf16[1024,16]{0,1:T(8,128)(2,1)S(1)} %copy-done.3), channel_id=1, source_target_pairs={{0,8},{8,16},{16,24},{24,32},{32,40},{40,48},{48,56},{56,64},{64,7... | collective-permute-start | bytes 98312 | tf_op jit(solution)/shard_map/ppermute | solution.py:34
  113.0 0.4 collective-permute-done.13
  113.4 1.8 collective-permute-done.14
  115.4 4.8 %collective-permute-start.15 = (bf16[1024,256]{0,1:T(8,128)(2,1)S(1)}, bf16[1024,256]{0,1:T(8,128)(2,1)S(1)}, u32[]{:S(2)}, u32[]{:S(2)}) collective-permute-start(bf16[1024,256]{0,1:T(8,128)(2,1)S(1)} %bitcast.143), channel_id=1, source_target_pairs={{0,384},{128,0},{256,128},{384,256},{1,385},{129,1},{257,129},{385... | collective-permute-start | bytes 1572872 | tf_op jit(solution)/shard_map/ppermute | solution.py:34
  120.3 0.1 convert_bitcast_fusion
  120.3 2.5 collective-permute-start.16
  122.9 0.1 broadcast_multiply_fusion
  123.0 2.9 %collective-permute-start.17 = (bf16[1024,256]{0,1:T(8,128)(2,1)S(1)}, bf16[1024,256]{0,1:T(8,128)(2,1)S(1)}, u32[]{:S(2)}, u32[]{:S(2)}) collective-permute-start(bf16[1024,256]{0,1:T(8,128)(2,1)S(1)} %bitcast.145), channel_id=1, source_target_pairs={{0,128},{128,256},{256,384},{384,0},{1,129},{129,257},{257,385},{3... | collective-permute-start | bytes 1572872 | tf_op jit(solution)/shard_map/ppermute | solution.py:34
  125.9 11.5 %collective-permute-done.15 = bf16[1024,256]{0,1:T(8,128)(2,1)S(1)} collective-permute-done((bf16[1024,256]{0,1:T(8,128)(2,1)S(1)}, bf16[1024,256]{0,1:T(8,128)(2,1)S(1)}, u32[]{:S(2)}, u32[]{:S(2)}) %collective-permute-start.15) | collective-permute-done | bytes 524320 | tf_op jit(solution)/shard_map/ppermute | solution.py:34
  137.5 0.1 collective-permute-done.16
  137.6 5.5 %collective-permute-done.17 = bf16[1024,256]{0,1:T(8,128)(2,1)S(1)} collective-permute-done((bf16[1024,256]{0,1:T(8,128)(2,1)S(1)}, bf16[1024,256]{0,1:T(8,128)(2,1)S(1)}, u32[]{:S(2)}, u32[]{:S(2)}) %collective-permute-start.17) | collective-permute-done | bytes 524320 | tf_op jit(solution)/shard_map/ppermute | solution.py:34
  143.3 1.5 constant_dynamic-slice_fusion
  144.9 0.2 convolution_multiply_fusion.2
  145.1 0.2 slice.20
  145.3 0.2 copy.77
  145.5 0.5 reshape.146
  146.0 0.4 convolution_bitcast_fusion.2
  146.4 22.7 %all-reduce.2 = (bf16[3,128,64]{1,2,0:T(8,128)(2,1)S(1)}, bf16[3,128,64]{1,2,0:T(8,128)(2,1)S(1)}) all-reduce(f32[3,128,64]{1,2,0:T(8,128)S(1)} %convolution_bitcast_fusion.2, f32[3,128,64]{1,2,0:T(8,128)S(1)} %convolution_multiply_fusion.2), channel_id=1, replica_groups=mesh['ay'=4,'az'=16,'mp'=8] {'mp'}, use_global_device_ids=true, to_apply=%region_2.3 | all-reduce | flops 49152 | bytes 294912 | tf_op jit(solution)/shard_map/psum | solution.py:105
  169.1 0.1 convolution_multiply_fusion.1
  169.2 1.2 convolution_bitcast_fusion.1
  170.4 1.6 copy.82
  172.0 1.3 reshape.151
  173.3 1.2 pad_maximum_fusion
  174.5 1.6 copy.83
  176.1 10.2 %all-to-all-start.1 = ((f32[3,64,1152]{2,0,1:T(4,128)}), f32[3,64,1152]{2,0,1:T(4,128)S(1)}, u32[]{:S(2)}, u32[]{:S(2)}) async-start(f32[3,64,1152]{2,0,1:T(4,128)} %copy.83), calls=%async_computation.2 | async-start | bytes 2359296 | tf_op jit(solution)/shard_map/all_to_all | solution.py:134
  186.3 0.0 reduce-scatter.2.cloned.1.call-start
  186.4 4.0 %convolution_bitcast_fusion = f32[384,1024]{0,1:T(8,128)} fusion(bf16[1024,1024]{0,1:T(8,128)(2,1)} %bitcast.150, bf16[384,1024]{1,0:T(8,128)(2,1)S(1)} %copy-done), kind=kOutput, calls=%fused_computation.4 | convolution fusion | flops 805306368 | bytes 4456448 | tf_op jit(solution)/shard_map/dot_general | solution.py:100
  190.4 0.0 reduce-scatter.2.cloned.1.call-update
  190.4 15.3 %all_gather.3 = bf16[384,1024]{1,0:T(8,128)(2,1)} all-gather(bf16[384,128]{1,0:T(8,128)(2,1)S(1)} %broadcast_multiply_fusion), channel_id=1, replica_groups=mesh['ay'=4,'az'=16,'mp'=8] {'mp'}, dimensions={1}, use_global_device_ids=true | all-gather | bytes 884736 | tf_op jit(solution)/shard_map/all_gather | solution.py:82
  205.7 0.2 convolution_multiply_fusion
  205.9 0.1 copy.80
  206.1 0.4 fusion.19
  206.5 3.7 %fusion = bf16[384,1024]{1,0:T(8,128)(2,1)} fusion(f32[3,128,1024]{2,1,0:T(8,128)S(1)} %fusion.19, bf16[384,1024]{1,0:T(8,128)(2,1)} %all_gather.3, bf16[1024,1024]{0,1:T(8,128)(2,1)} %bitcast.151), kind=kOutput, calls=%fused_computation.3 | convolution fusion | flops 806092800 | bytes 5242880 | tf_op jit(solution)/shard_map/dot_general | solution.py:118
  210.2 19.9 %reduce-scatter.2.cloned.1.call-done = f32[384,128]{0,1:T(8,128)} async-done(((f32[384,1024]{0,1:T(8,128)}), f32[384,128]{0,1:T(8,128)}) %reduce-scatter.2.cloned.1.call-update) | async-done | bytes 196624 | tf_op jit(solution)/shard_map/reduce_scatter | solution.py:101
  230.1 1.0 multiply_convert_fusion
  231.0 0.8 copy.87
  231.8 14.7 %all-to-all-done.1 = f32[3,64,1152]{2,0,1:T(4,128)S(1)} async-done(((f32[3,64,1152]{2,0,1:T(4,128)}), f32[3,64,1152]{2,0,1:T(4,128)S(1)}, u32[]{:S(2)}, u32[]{:S(2)}) %all-to-all-start.1) | async-done | bytes 884768 | tf_op jit(solution)/shard_map/all_to_all | solution.py:134
  246.5 2.1 all_to_all.21
  248.6 1.7 slice.22
  250.3 1.0 fusion.1
  251.3 2.6 divide_subtract_fusion
  254.0 0.9 divide_subtract_fusion.1
  (77 shorter events, 0.6 us)
Async XLA Ops:
  7.2 138.8 %copy-start = (bf16[384,1024]{1,0:T(8,128)(2,1)S(1)}, bf16[384,1024]{1,0:T(8,128)(2,1)}, u32[]{:S(2)}) copy-start(bf16[384,1024]{1,0:T(8,128)(2,1)} %param.12) | copy-start | bytes 2359300
  7.2 46.7 %copy-start.3 = (bf16[1024,16]{0,1:T(8,128)(2,1)S(1)}, bf16[1024,16]{0,1:T(8,128)(2,1)}, u32[]{:S(2)}) copy-start(bf16[1024,16]{0,1:T(8,128)(2,1)} %param.14) | copy-start | bytes 98308
  7.2 46.7 %copy-start.7 = (s32[192]{0:T(256)S(1)}, s32[192]{0:T(256)}, u32[]{:S(2)}) copy-start(s32[192]{0:T(256)} %param.22) | copy-start | bytes 2308
  7.2 46.8 %collective-permute-start = (bf16[1024,16]{0,1:T(8,128)(2,1)}, bf16[1024,16]{0,1:T(8,128)(2,1)S(1)}, u32[]{:S(2)}, u32[]{:S(2)}) collective-permute-start(bf16[1024,16]{0,1:T(8,128)(2,1)} %param.14), channel_id=1, source_target_pairs={{0,120},{8,0},{16,8},{24,16},{32,24},{40,32},{48,40},{56,48},{64,5... | collective-permute-start | bytes 98312 | tf_op jit(solution)/shard_map/ppermute | solution.py:34
  18.7 45.6 %collective-permute-start.1 = (bf16[1024,16]{0,1:T(8,128)(2,1)}, bf16[1024,16]{0,1:T(8,128)(2,1)S(1)}, u32[]{:S(2)}, u32[]{:S(2)}) collective-permute-start(bf16[1024,16]{0,1:T(8,128)(2,1)} %param.14), channel_id=1, source_target_pairs={{0,112},{8,120},{16,0},{24,8},{32,16},{40,24},{48,32},{56,40},{64,... | collective-permute-start | bytes 98312 | tf_op jit(solution)/shard_map/ppermute | solution.py:34
  22.1 46.6 %collective-permute-start.2 = (bf16[1024,16]{0,1:T(8,128)(2,1)}, bf16[1024,16]{0,1:T(8,128)(2,1)S(1)}, u32[]{:S(2)}, u32[]{:S(2)}) collective-permute-start(bf16[1024,16]{0,1:T(8,128)(2,1)} %param.14), channel_id=1, source_target_pairs={{0,104},{8,112},{16,120},{24,0},{32,8},{40,16},{48,24},{56,32},{64... | collective-permute-start | bytes 98312 | tf_op jit(solution)/shard_map/ppermute | solution.py:34
  27.1 51.0 %collective-permute-start.3 = (bf16[1024,16]{0,1:T(8,128)(2,1)}, bf16[1024,16]{0,1:T(8,128)(2,1)S(1)}, u32[]{:S(2)}, u32[]{:S(2)}) collective-permute-start(bf16[1024,16]{0,1:T(8,128)(2,1)} %param.14), channel_id=1, source_target_pairs={{0,96},{8,104},{16,112},{24,120},{32,0},{40,8},{48,16},{56,24},{64... | collective-permute-start | bytes 98312 | tf_op jit(solution)/shard_map/ppermute | solution.py:34
  30.0 51.2 %collective-permute-start.4 = (bf16[1024,16]{0,1:T(8,128)(2,1)}, bf16[1024,16]{0,1:T(8,128)(2,1)S(1)}, u32[]{:S(2)}, u32[]{:S(2)}) collective-permute-start(bf16[1024,16]{0,1:T(8,128)(2,1)} %param.14), channel_id=1, source_target_pairs={{0,88},{8,96},{16,104},{24,112},{32,120},{40,0},{48,8},{56,16},{64... | collective-permute-start | bytes 98312 | tf_op jit(solution)/shard_map/ppermute | solution.py:34
  34.2 88.7 %copy-start.4 = (bf16[384,128]{1,0:T(8,128)(2,1)S(1)}, bf16[384,128]{1,0:T(8,128)(2,1)}, u32[]{:S(2)}) copy-start(bf16[384,128]{1,0:T(8,128)(2,1)} %param.13) | copy-start | bytes 294916
  38.1 106.8 %all-to-all-start = ((bf16[64,3,1152]{2,1,0:T(4,128)(2,1)}), bf16[64,3,1152]{2,1,0:T(4,128)(2,1)S(1)}, u32[]{:S(2)}, u32[]{:S(2)}) async-start(bf16[64,3,1152]{2,1,0:T(4,128)(2,1)} %pad_maximum_fusion.1), calls=%async_computation.1 | async-start | bytes 1179648 | tf_op jit(solution)/shard_map/all_to_all | solution.py:89
  54.0 37.5 %collective-permute-start.5 = (bf16[1024,16]{0,1:T(8,128)(2,1)S(1)}, bf16[1024,16]{0,1:T(8,128)(2,1)S(1)}, u32[]{:S(2)}, u32[]{:S(2)}) collective-permute-start(bf16[1024,16]{0,1:T(8,128)(2,1)S(1)} %copy-done.3), channel_id=1, source_target_pairs={{0,80},{8,88},{16,96},{24,104},{32,112},{40,120},{48,0},{56,8},{64... | collective-permute-start | bytes 98312 | tf_op jit(solution)/shard_map/ppermute | solution.py:34
  64.4 33.8 %collective-permute-start.6 = (bf16[1024,16]{0,1:T(8,128)(2,1)S(1)}, bf16[1024,16]{0,1:T(8,128)(2,1)S(1)}, u32[]{:S(2)}, u32[]{:S(2)}) collective-permute-start(bf16[1024,16]{0,1:T(8,128)(2,1)S(1)} %copy-done.3), channel_id=1, source_target_pairs={{0,72},{8,80},{16,88},{24,96},{32,104},{40,112},{48,120},{56,0},{6... | collective-permute-start | bytes 98312 | tf_op jit(solution)/shard_map/ppermute | solution.py:34
  68.7 31.5 %collective-permute-start.7 = (bf16[1024,16]{0,1:T(8,128)(2,1)S(1)}, bf16[1024,16]{0,1:T(8,128)(2,1)S(1)}, u32[]{:S(2)}, u32[]{:S(2)}) collective-permute-start(bf16[1024,16]{0,1:T(8,128)(2,1)S(1)} %copy-done.3), channel_id=1, source_target_pairs={{0,64},{8,72},{16,80},{24,88},{32,96},{40,104},{48,112},{56,120},{... | collective-permute-start | bytes 98312 | tf_op jit(solution)/shard_map/ppermute | solution.py:34
  78.1 27.3 %collective-permute-start.8 = (bf16[1024,16]{0,1:T(8,128)(2,1)S(1)}, bf16[1024,16]{0,1:T(8,128)(2,1)S(1)}, u32[]{:S(2)}, u32[]{:S(2)}) collective-permute-start(bf16[1024,16]{0,1:T(8,128)(2,1)S(1)} %copy-done.3), channel_id=1, source_target_pairs={{0,56},{8,64},{16,72},{24,80},{32,88},{40,96},{48,104},{56,112},{6... | collective-permute-start | bytes 98312 | tf_op jit(solution)/shard_map/ppermute | solution.py:34
  81.2 26.9 %collective-permute-start.9 = (bf16[1024,16]{0,1:T(8,128)(2,1)S(1)}, bf16[1024,16]{0,1:T(8,128)(2,1)S(1)}, u32[]{:S(2)}, u32[]{:S(2)}) collective-permute-start(bf16[1024,16]{0,1:T(8,128)(2,1)S(1)} %copy-done.3), channel_id=1, source_target_pairs={{0,48},{8,56},{16,64},{24,72},{32,80},{40,88},{48,96},{56,104},{64... | collective-permute-start | bytes 98312 | tf_op jit(solution)/shard_map/ppermute | solution.py:34
  91.5 21.4 %collective-permute-start.10 = (bf16[1024,16]{0,1:T(8,128)(2,1)S(1)}, bf16[1024,16]{0,1:T(8,128)(2,1)S(1)}, u32[]{:S(2)}, u32[]{:S(2)}) collective-permute-start(bf16[1024,16]{0,1:T(8,128)(2,1)S(1)} %copy-done.3), channel_id=1, source_target_pairs={{0,40},{8,48},{16,56},{24,64},{32,72},{40,80},{48,88},{56,96},{64,... | collective-permute-start | bytes 98312 | tf_op jit(solution)/shard_map/ppermute | solution.py:34
  98.2 14.7 %collective-permute-start.11 = (bf16[1024,16]{0,1:T(8,128)(2,1)S(1)}, bf16[1024,16]{0,1:T(8,128)(2,1)S(1)}, u32[]{:S(2)}, u32[]{:S(2)}) collective-permute-start(bf16[1024,16]{0,1:T(8,128)(2,1)S(1)} %copy-done.3), channel_id=1, source_target_pairs={{0,32},{8,40},{16,48},{24,56},{32,64},{40,72},{48,80},{56,88},{64,... | collective-permute-start | bytes 98312 | tf_op jit(solution)/shard_map/ppermute | solution.py:34
  100.2 12.8 %collective-permute-start.12 = (bf16[1024,16]{0,1:T(8,128)(2,1)S(1)}, bf16[1024,16]{0,1:T(8,128)(2,1)S(1)}, u32[]{:S(2)}, u32[]{:S(2)}) collective-permute-start(bf16[1024,16]{0,1:T(8,128)(2,1)S(1)} %copy-done.3), channel_id=1, source_target_pairs={{0,24},{8,32},{16,40},{24,48},{32,56},{40,64},{48,72},{56,80},{64,... | collective-permute-start | bytes 98312 | tf_op jit(solution)/shard_map/ppermute | solution.py:34
  105.5 7.9 %collective-permute-start.13 = (bf16[1024,16]{0,1:T(8,128)(2,1)S(1)}, bf16[1024,16]{0,1:T(8,128)(2,1)S(1)}, u32[]{:S(2)}, u32[]{:S(2)}) collective-permute-start(bf16[1024,16]{0,1:T(8,128)(2,1)S(1)} %copy-done.3), channel_id=1, source_target_pairs={{0,16},{8,24},{16,32},{24,40},{32,48},{40,56},{48,64},{56,72},{64,... | collective-permute-start | bytes 98312 | tf_op jit(solution)/shard_map/ppermute | solution.py:34
  108.1 7.0 %collective-permute-start.14 = (bf16[1024,16]{0,1:T(8,128)(2,1)S(1)}, bf16[1024,16]{0,1:T(8,128)(2,1)S(1)}, u32[]{:S(2)}, u32[]{:S(2)}) collective-permute-start(bf16[1024,16]{0,1:T(8,128)(2,1)S(1)} %copy-done.3), channel_id=1, source_target_pairs={{0,8},{8,16},{16,24},{24,32},{32,40},{40,48},{48,56},{56,64},{64,7... | collective-permute-start | bytes 98312 | tf_op jit(solution)/shard_map/ppermute | solution.py:34
  115.4 22.0 %collective-permute-start.15 = (bf16[1024,256]{0,1:T(8,128)(2,1)S(1)}, bf16[1024,256]{0,1:T(8,128)(2,1)S(1)}, u32[]{:S(2)}, u32[]{:S(2)}) collective-permute-start(bf16[1024,256]{0,1:T(8,128)(2,1)S(1)} %bitcast.143), channel_id=1, source_target_pairs={{0,384},{128,0},{256,128},{384,256},{1,385},{129,1},{257,129},{385... | collective-permute-start | bytes 1572872 | tf_op jit(solution)/shard_map/ppermute | solution.py:34
  120.3 17.2 %collective-permute-start.16 = (bf16[1024,256]{0,1:T(8,128)(2,1)S(1)}, bf16[1024,256]{0,1:T(8,128)(2,1)S(1)}, u32[]{:S(2)}, u32[]{:S(2)}) collective-permute-start(bf16[1024,256]{0,1:T(8,128)(2,1)S(1)} %bitcast.144), channel_id=1, source_target_pairs={{0,256},{128,384},{256,0},{384,128},{1,257},{129,385},{257,1},{385... | collective-permute-start | bytes 1572872 | tf_op jit(solution)/shard_map/ppermute | solution.py:34
  123.0 20.1 %collective-permute-start.17 = (bf16[1024,256]{0,1:T(8,128)(2,1)S(1)}, bf16[1024,256]{0,1:T(8,128)(2,1)S(1)}, u32[]{:S(2)}, u32[]{:S(2)}) collective-permute-start(bf16[1024,256]{0,1:T(8,128)(2,1)S(1)} %bitcast.145), channel_id=1, source_target_pairs={{0,128},{128,256},{256,384},{384,0},{1,129},{129,257},{257,385},{3... | collective-permute-start | bytes 1572872 | tf_op jit(solution)/shard_map/ppermute | solution.py:34
  176.1 70.4 %all-to-all-start.1 = ((f32[3,64,1152]{2,0,1:T(4,128)}), f32[3,64,1152]{2,0,1:T(4,128)S(1)}, u32[]{:S(2)}, u32[]{:S(2)}) async-start(f32[3,64,1152]{2,0,1:T(4,128)} %copy.83), calls=%async_computation.2 | async-start | bytes 2359296 | tf_op jit(solution)/shard_map/all_to_all | solution.py:134
  186.3 43.7 %reduce-scatter.2.cloned.1.call-start = ((), (), s32[]{:S(2)}) async-start(), calls=%async_computation.3 | async-start | bytes 1769472 | tf_op jit(solution)/shard_map/reduce_scatter | solution.py:101
  210.2 41.1 %copy-start.2 = (bf16[128,1,16,64]{0,3,2,1:T(8,128)(2,1)S(1)}, bf16[128,1,16,64]{0,3,2,1:T(8,128)(2,1)}, u32[]{:S(2)}) copy-start(bf16[128,1,16,64]{0,3,2,1:T(8,128)(2,1)} %param.15) | copy-start | bytes 786436
  246.5 7.4 %copy-start.1 = (bf16[128,1,128]{2,0,1:T(8,128)(2,1)S(1)}, bf16[128,1,128]{2,0,1:T(8,128)(2,1)}, u32[]{:S(2)}) copy-start(bf16[128,1,128]{2,0,1:T(8,128)(2,1)} %param.18) | copy-start | bytes 98308
  246.5 7.4 %copy-start.5 = (f32[128,1,128]{2,1,0:T(1,128)S(1)}, f32[128,1,128]{2,1,0:T(1,128)}, u32[]{:S(2)}) copy-start(f32[128,1,128]{2,1,0:T(1,128)} %param.19) | copy-start | bytes 196612
  246.5 7.4 %copy-start.6 = (f32[128,1,128]{2,1,0:T(1,128)S(1)}, f32[128,1,128]{2,1,0:T(1,128)}, u32[]{:S(2)}) copy-start(f32[128,1,128]{2,1,0:T(1,128)} %param.20) | copy-start | bytes 196612
  248.6 5.4 %slice-start = ((f32[192,1,1152]{2,1,0:T(1,128)}), f32[192,1,128]{2,1,0:T(1,128)S(1)}, s32[]{:S(2)}) async-start(f32[192,1,1152]{2,1,0:T(1,128)} %all_to_all.21), calls=%async_computation.4 | async-start | bytes 196608 | tf_op jit(solution)/shard_map/slice | solution.py:136
Sparse Core Ops, SparseCore 0:
  190.5 39.4 reduce-scatter.1
where the time goes:
time: 263 us; the launch traced here: 262 us
  starting transfers between devices  120 us (46%)
  waiting for transfers between devices  54 us (21%)
  blocking collectives  38 us (14%)
  local copies, waits for them, and re-layouts  16.4 us (6%)
  between operations  14.8 us (6%)
  matrix products  12.2 us (5%)
  other arithmetic  6.9 us (3%)
    ppermute x18, starting transfers between devices, gather_along(): got.append(lax.ppermute(piece, axis, pairs))  93.5 us
    psum x1, blocking collectives, shards(): down_sum = lax.psum(down_part, 'mp')  22.7 us
    reduce_scatter x1, waiting for transfers between devices, shards(): lax.psum_scatter(frozen_part, 'mp', scatter_dimension=1, tiled=True)  19.9 us
    ppermute x18, waiting for transfers between devices, gather_along(): got.append(lax.ppermute(piece, axis, pairs))  19.3 us
    all_to_all x1, starting transfers between devices, shards(): lax.all_to_all(sent, ADAPTER, split_axis=0, concat_axis=0, tiled=True)  15.8 us
    all_gather x1, blocking collectives, shards(): masked_full = lax.all_gather(masked_own, 'mp', axis=1, tiled=True)  15.3 us
    all_to_all x1, waiting for transfers between devices, shards(): lax.all_to_all(grads, ADAPTER, split_axis=1, concat_axis=0, tiled=True)  14.7 us
    all_to_all x1, starting transfers between devices, shards(): lax.all_to_all(grads, ADAPTER, split_axis=1, concat_axis=0, tiled=True)  10.2 us
  transfers between devices with their start and end apart: 21, of which 7 were waited for; matrix products, arithmetic and copies ran while one was open for 7% of the time, Pallas kernels for 0%

commit v1 on v0

--- a/solution.py
+++ b/solution.py
@@ -79,7 +79,9 @@
     my_lengths = lax.dynamic_slice_in_dim(tile_length, my_index * tiles_here, tiles_here)
     active_rows = (jnp.arange(TILE)[None, :] < my_lengths[:, None]).reshape(tok_count, 1)
     masked_own = cotangent * active_rows.astype(jnp.bfloat16)
-    masked_full = lax.all_gather(masked_own, "mp", axis=1, tiled=True)
+    masked_full = jnp.concatenate(
+        lax.all_to_all(jnp.stack([masked_own] * lax.axis_size("mp")), "mp", 0, 0), axis=1
+    )
     n_adapter = tile_total // tiles_here
     row_part = down_store.shape[2]
     rank = down_store.shape[3]

time: 263 us -> 276 us (1.049)
  waiting for transfers between devices: 54 us -> 68.4 us
  blocking collectives: 38 us -> 25.3 us
  starting transfers between devices: 120 us -> 125 us
  local copies, waits for them, and re-layouts: 16.4 us -> 20.2 us
    reduce_scatter x1, waiting for transfers between devices: 19.9 us -> 35.5 us  [shards(): lax.psum_scatter(frozen_part, 'mp', scatter_dimension=1, tiled=True)]
    all_gather x1 -> x0, blocking collectives: 15.3 us -> none  [shards(): masked_full = lax.all_gather(masked_own, 'mp', axis=1, tiled=True)]
    all_to_all x0 -> x1, starting transfers between devices: none -> 4.78 us  [shards(): lax.all_to_all(jnp.stack([masked_own] * lax.axis_size('mp')), 'mp', 0, 0)]
  transfers between devices with their start and end apart: 21 -> 22, of which waited for: 7 -> 7; matrix products, arithmetic and copies ran while one was open for 7% -> 12% of each run, Pallas kernels for 0% -> 0%
where the time goes in v1:
time: 276 us; the launch traced here: 274 us
  starting transfers between devices  125 us (45%)
  waiting for transfers between devices  68.4 us (25%)
  blocking collectives  25.3 us (9%)
  local copies, waits for them, and re-layouts  20.2 us (7%)
  between operations  14.8 us (5%)
  matrix products  13.8 us (5%)
  other arithmetic  6.6 us (2%)
    ppermute x18, starting transfers between devices, gather_along(): got.append(lax.ppermute(piece, axis, pairs))  93.5 us
    reduce_scatter x1, waiting for transfers between devices, shards(): lax.psum_scatter(frozen_part, 'mp', scatter_dimension=1, tiled=True)  35.5 us
    psum x1, blocking collectives, shards(): down_sum = lax.psum(down_part, 'mp')  25.3 us
    ppermute x18, waiting for transfers between devices, gather_along(): got.append(lax.ppermute(piece, axis, pairs))  17.7 us
    all_to_all x1, starting transfers between devices, shards(): lax.all_to_all(sent, ADAPTER, split_axis=0, concat_axis=0, tiled=True)  15.8 us
    all_to_all x1, waiting for transfers between devices, shards(): lax.all_to_all(grads, ADAPTER, split_axis=1, concat_axis=0, tiled=True)  15.2 us
    all_to_all x1, starting transfers between devices, shards(): lax.all_to_all(grads, ADAPTER, split_axis=1, concat_axis=0, tiled=True)  10.6 us
  transfers between devices with their start and end apart: 22, of which 7 were waited for; matrix products, arithmetic and copies ran while one was open for 12% of the time, Pallas kernels for 0%

profile of v1, /device:TPU:6, one launch (start us, length us, event | category | flops | bytes accessed | tf_op | source)
XLA Modules:
  0.0 274.1 jit_solution(9231686534893310610)
XLA Ops:
  7.2 11.5 %collective-permute-start = (bf16[1024,16]{0,1:T(8,128)(2,1)}, bf16[1024,16]{0,1:T(8,128)(2,1)S(1)}, u32[]{:S(2)}, u32[]{:S(2)}) collective-permute-start(bf16[1024,16]{0,1:T(8,128)(2,1)} %param.14), channel_id=1, source_target_pairs={{0,120},{8,0},{16,8},{24,16},{32,24},{40,32},{48,40},{56,48},{64,5... | collective-permute-start | bytes 98312 | tf_op jit(solution)/shard_map/ppermute | solution.py:34
  18.7 3.4 %collective-permute-start.1 = (bf16[1024,16]{0,1:T(8,128)(2,1)}, bf16[1024,16]{0,1:T(8,128)(2,1)S(1)}, u32[]{:S(2)}, u32[]{:S(2)}) collective-permute-start(bf16[1024,16]{0,1:T(8,128)(2,1)} %param.14), channel_id=1, source_target_pairs={{0,112},{8,120},{16,0},{24,8},{32,16},{40,24},{48,32},{56,40},{64,... | collective-permute-start | bytes 98312 | tf_op jit(solution)/shard_map/ppermute | solution.py:34
  22.1 5.0 %collective-permute-start.2 = (bf16[1024,16]{0,1:T(8,128)(2,1)}, bf16[1024,16]{0,1:T(8,128)(2,1)S(1)}, u32[]{:S(2)}, u32[]{:S(2)}) collective-permute-start(bf16[1024,16]{0,1:T(8,128)(2,1)} %param.14), channel_id=1, source_target_pairs={{0,104},{8,112},{16,120},{24,0},{32,8},{40,16},{48,24},{56,32},{64... | collective-permute-start | bytes 98312 | tf_op jit(solution)/shard_map/ppermute | solution.py:34
  27.1 2.8 %collective-permute-start.3 = (bf16[1024,16]{0,1:T(8,128)(2,1)}, bf16[1024,16]{0,1:T(8,128)(2,1)S(1)}, u32[]{:S(2)}, u32[]{:S(2)}) collective-permute-start(bf16[1024,16]{0,1:T(8,128)(2,1)} %param.14), channel_id=1, source_target_pairs={{0,96},{8,104},{16,112},{24,120},{32,0},{40,8},{48,16},{56,24},{64... | collective-permute-start | bytes 98312 | tf_op jit(solution)/shard_map/ppermute | solution.py:34
  30.0 1.9 collective-permute-start.4
  31.9 0.9 select_reduce_fusion
  32.8 1.4 copy.79
  34.2 0.8 gather_fusion
  35.0 0.5 concatenate.23
  35.5 1.5 gather_fusion.1
  37.0 1.1 pad_maximum_fusion.1
  38.1 15.8 %all-to-all-start = ((bf16[64,3,1152]{2,1,0:T(4,128)(2,1)}), bf16[64,3,1152]{2,1,0:T(4,128)(2,1)S(1)}, u32[]{:S(2)}, u32[]{:S(2)}) async-start(bf16[64,3,1152]{2,1,0:T(4,128)(2,1)} %pad_maximum_fusion.1), calls=%async_computation.1 | async-start | bytes 1179648 | tf_op jit(solution)/shard_map/all_to_all | solution.py:91
  53.9 0.1 dynamic_slice.13
  54.0 10.4 %collective-permute-start.5 = (bf16[1024,16]{0,1:T(8,128)(2,1)S(1)}, bf16[1024,16]{0,1:T(8,128)(2,1)S(1)}, u32[]{:S(2)}, u32[]{:S(2)}) collective-permute-start(bf16[1024,16]{0,1:T(8,128)(2,1)S(1)} %copy-done.7), channel_id=1, source_target_pairs={{0,80},{8,88},{16,96},{24,104},{32,112},{40,120},{48,0},{56,8},{64... | collective-permute-start | bytes 98312 | tf_op jit(solution)/shard_map/ppermute | solution.py:34
  64.4 4.3 %collective-permute-start.6 = (bf16[1024,16]{0,1:T(8,128)(2,1)S(1)}, bf16[1024,16]{0,1:T(8,128)(2,1)S(1)}, u32[]{:S(2)}, u32[]{:S(2)}) collective-permute-start(bf16[1024,16]{0,1:T(8,128)(2,1)S(1)} %copy-done.7), channel_id=1, source_target_pairs={{0,72},{8,80},{16,88},{24,96},{32,104},{40,112},{48,120},{56,0},{6... | collective-permute-start | bytes 98312 | tf_op jit(solution)/shard_map/ppermute | solution.py:34
  68.7 9.4 %collective-permute-start.7 = (bf16[1024,16]{0,1:T(8,128)(2,1)S(1)}, bf16[1024,16]{0,1:T(8,128)(2,1)S(1)}, u32[]{:S(2)}, u32[]{:S(2)}) collective-permute-start(bf16[1024,16]{0,1:T(8,128)(2,1)S(1)} %copy-done.7), channel_id=1, source_target_pairs={{0,64},{8,72},{16,80},{24,88},{32,96},{40,104},{48,112},{56,120},{... | collective-permute-start | bytes 98312 | tf_op jit(solution)/shard_map/ppermute | solution.py:34
  78.1 3.1 %collective-permute-start.8 = (bf16[1024,16]{0,1:T(8,128)(2,1)S(1)}, bf16[1024,16]{0,1:T(8,128)(2,1)S(1)}, u32[]{:S(2)}, u32[]{:S(2)}) collective-permute-start(bf16[1024,16]{0,1:T(8,128)(2,1)S(1)} %copy-done.7), channel_id=1, source_target_pairs={{0,56},{8,64},{16,72},{24,80},{32,88},{40,96},{48,104},{56,112},{6... | collective-permute-start | bytes 98312 | tf_op jit(solution)/shard_map/ppermute | solution.py:34
  81.2 10.3 %collective-permute-start.9 = (bf16[1024,16]{0,1:T(8,128)(2,1)S(1)}, bf16[1024,16]{0,1:T(8,128)(2,1)S(1)}, u32[]{:S(2)}, u32[]{:S(2)}) collective-permute-start(bf16[1024,16]{0,1:T(8,128)(2,1)S(1)} %copy-done.7), channel_id=1, source_target_pairs={{0,48},{8,56},{16,64},{24,72},{32,80},{40,88},{48,96},{56,104},{64... | collective-permute-start | bytes 98312 | tf_op jit(solution)/shard_map/ppermute | solution.py:34
  91.5 6.7 %collective-permute-start.10 = (bf16[1024,16]{0,1:T(8,128)(2,1)S(1)}, bf16[1024,16]{0,1:T(8,128)(2,1)S(1)}, u32[]{:S(2)}, u32[]{:S(2)}) collective-permute-start(bf16[1024,16]{0,1:T(8,128)(2,1)S(1)} %copy-done.7), channel_id=1, source_target_pairs={{0,40},{8,48},{16,56},{24,64},{32,72},{40,80},{48,88},{56,96},{64,... | collective-permute-start | bytes 98312 | tf_op jit(solution)/shard_map/ppermute | solution.py:34
  98.2 1.9 collective-permute-start.11
  100.2 5.2 %collective-permute-start.12 = (bf16[1024,16]{0,1:T(8,128)(2,1)S(1)}, bf16[1024,16]{0,1:T(8,128)(2,1)S(1)}, u32[]{:S(2)}, u32[]{:S(2)}) collective-permute-start(bf16[1024,16]{0,1:T(8,128)(2,1)S(1)} %copy-done.7), channel_id=1, source_target_pairs={{0,24},{8,32},{16,40},{24,48},{32,56},{40,64},{48,72},{56,80},{64,... | collective-permute-start | bytes 98312 | tf_op jit(solution)/shard_map/ppermute | solution.py:34
  105.4 2.7 collective-permute-start.13
  108.1 4.8 %collective-permute-start.14 = (bf16[1024,16]{0,1:T(8,128)(2,1)S(1)}, bf16[1024,16]{0,1:T(8,128)(2,1)S(1)}, u32[]{:S(2)}, u32[]{:S(2)}) collective-permute-start(bf16[1024,16]{0,1:T(8,128)(2,1)S(1)} %copy-done.7), channel_id=1, source_target_pairs={{0,8},{8,16},{16,24},{24,32},{32,40},{40,48},{48,56},{56,64},{64,7... | collective-permute-start | bytes 98312 | tf_op jit(solution)/shard_map/ppermute | solution.py:34
  113.0 0.4 collective-permute-done.13
  113.4 1.8 collective-permute-done.14
  115.4 4.8 %collective-permute-start.15 = (bf16[1024,256]{0,1:T(8,128)(2,1)S(1)}, bf16[1024,256]{0,1:T(8,128)(2,1)S(1)}, u32[]{:S(2)}, u32[]{:S(2)}) collective-permute-start(bf16[1024,256]{0,1:T(8,128)(2,1)S(1)} %bitcast.147), channel_id=1, source_target_pairs={{0,384},{128,0},{256,128},{384,256},{1,385},{129,1},{257,129},{385... | collective-permute-start | bytes 1572872 | tf_op jit(solution)/shard_map/ppermute | solution.py:34
  120.2 0.1 convert_bitcast_fusion
  120.3 2.5 collective-permute-start.16
  122.9 1.0 broadcast_multiply_fusion
  123.9 0.8 copy.84
  124.6 2.9 %collective-permute-start.17 = (bf16[1024,256]{0,1:T(8,128)(2,1)S(1)}, bf16[1024,256]{0,1:T(8,128)(2,1)S(1)}, u32[]{:S(2)}, u32[]{:S(2)}) collective-permute-start(bf16[1024,256]{0,1:T(8,128)(2,1)S(1)} %bitcast.149), channel_id=1, source_target_pairs={{0,128},{128,256},{256,384},{384,0},{1,129},{129,257},{257,385},{3... | collective-permute-start | bytes 1572872 | tf_op jit(solution)/shard_map/ppermute | solution.py:34
  127.6 9.9 %collective-permute-done.15 = bf16[1024,256]{0,1:T(8,128)(2,1)S(1)} collective-permute-done((bf16[1024,256]{0,1:T(8,128)(2,1)S(1)}, bf16[1024,256]{0,1:T(8,128)(2,1)S(1)}, u32[]{:S(2)}, u32[]{:S(2)}) %collective-permute-start.15) | collective-permute-done | bytes 524320 | tf_op jit(solution)/shard_map/ppermute | solution.py:34
  137.6 5.5 %collective-permute-done.17 = bf16[1024,256]{0,1:T(8,128)(2,1)S(1)} collective-permute-done((bf16[1024,256]{0,1:T(8,128)(2,1)S(1)}, bf16[1024,256]{0,1:T(8,128)(2,1)S(1)}, u32[]{:S(2)}, u32[]{:S(2)}) %collective-permute-start.17) | collective-permute-done | bytes 524320 | tf_op jit(solution)/shard_map/ppermute | solution.py:34
  143.3 0.2 constant_dynamic-slice_fusion
  143.5 1.8 stack.89
  145.4 4.8 %all-to-all-start.1 = ((bf16[8,384,128]{1,2,0:T(8,128)(2,1)}), bf16[8,384,128]{1,2,0:T(8,128)(2,1)}, u32[]{:S(2)}, u32[]{:S(2)}) async-start(bf16[8,384,128]{1,2,0:T(8,128)(2,1)} %stack.89), calls=%async_computation.2 | async-start | bytes 1572864 | tf_op jit(solution)/shard_map/all_to_all | solution.py:83
  150.2 1.7 convolution_multiply_fusion.2
  151.9 0.2 slice.20
  152.1 0.2 copy.80
  152.3 1.4 reshape.154
  153.6 1.6 convolution_bitcast_fusion.2
  155.2 25.3 %all-reduce.2 = (bf16[3,128,64]{1,2,0:T(8,128)(2,1)S(1)}, bf16[3,128,64]{1,2,0:T(8,128)(2,1)S(1)}) all-reduce(f32[3,128,64]{1,2,0:T(8,128)S(1)} %convolution_bitcast_fusion.2, f32[3,128,64]{1,2,0:T(8,128)} %convolution_multiply_fusion.2), channel_id=1, replica_groups=mesh['ay'=4,'az'=16,'mp'=8] {'mp'}, use_global_device_ids=true, to_apply=%region_2.3 | all-reduce | flops 49152 | bytes 294912 | tf_op jit(solution)/shard_map/psum | solution.py:107
  180.6 1.2 convolution_bitcast_fusion.1
  181.8 2.8 %copy.86 = f32[3,1024,64]{2,1,0:T(8,128)} copy(f32[3,1024,64]{1,2,0:T(8,128)} %convolution_bitcast_fusion.1) | data formatting | bytes 1572864 | tf_op jit(solution)/shard_map/ntd,ntr->ndr/dot_general | solution.py:127
  184.6 2.7 reshape.161
  187.2 0.1 convolution_multiply_fusion.1
  187.4 1.2 pad_maximum_fusion
  188.6 1.6 copy.87
  190.3 10.6 %all-to-all-start.2 = ((f32[3,64,1152]{2,0,1:T(4,128)}), f32[3,64,1152]{2,0,1:T(4,128)}, u32[]{:S(2)}, u32[]{:S(2)}) async-start(f32[3,64,1152]{2,0,1:T(4,128)} %copy.87), calls=%async_computation.3 | async-start | bytes 2359296 | tf_op jit(solution)/shard_map/all_to_all | solution.py:136
  200.9 0.2 reduce-scatter.2.cloned.1.call-start
  201.1 2.5 convolution_bitcast_fusion
  203.6 0.2 convolution_multiply_fusion
  203.8 0.1 copy.83
  203.9 1.6 fusion.19
  205.5 3.0 %fusion = bf16[384,1024]{1,0:T(8,128)(2,1)} fusion(f32[3,128,1024]{2,1,0:T(8,128)S(1)} %fusion.19, bf16[384,1024]{0,1:T(8,128)(2,1)} %bitcast.39, bf16[1024,1024]{0,1:T(8,128)(2,1)S(1)} %bitcast.143), kind=kOutput, calls=%fused_computation.3 | convolution fusion | flops 806092800 | bytes 5242880 | tf_op jit(solution)/shard_map/dot_general | solution.py:120
  208.5 35.5 %reduce-scatter.2.cloned.1.call-done = f32[384,128]{0,1:T(8,128)} async-done(((f32[384,1024]{0,1:T(8,128)}), f32[384,128]{0,1:T(8,128)}) %reduce-scatter.2.cloned.1.call-update) | async-done | bytes 196624 | tf_op jit(solution)/shard_map/reduce_scatter | solution.py:103
  244.0 1.0 multiply_convert_fusion
  245.0 0.8 copy.91
  245.7 15.2 %all-to-all-done.2 = f32[3,64,1152]{2,0,1:T(4,128)} async-done(((f32[3,64,1152]{2,0,1:T(4,128)}), f32[3,64,1152]{2,0,1:T(4,128)}, u32[]{:S(2)}, u32[]{:S(2)}) %all-to-all-start.2) | async-done | bytes 884768 | tf_op jit(solution)/shard_map/all_to_all | solution.py:136
  260.9 2.3 all_to_all.25
  263.3 0.5 slice.22
  263.9 1.0 fusion.1
  265.0 1.4 divide_subtract_fusion
  266.4 0.9 divide_subtract_fusion.1
  (85 shorter events, 0.8 us)
Async XLA Ops:
  7.2 146.5 %copy-start = (bf16[384,1024]{1,0:T(8,128)(2,1)S(1)}, bf16[384,1024]{1,0:T(8,128)(2,1)}, u32[]{:S(2)}) copy-start(bf16[384,1024]{1,0:T(8,128)(2,1)} %param.12) | copy-start | bytes 2359300
  7.2 46.6 %copy-start.7 = (bf16[1024,16]{0,1:T(8,128)(2,1)S(1)}, bf16[1024,16]{0,1:T(8,128)(2,1)}, u32[]{:S(2)}) copy-start(bf16[1024,16]{0,1:T(8,128)(2,1)} %param.14) | copy-start | bytes 98308
  7.2 46.7 %copy-start.10 = (s32[192]{0:T(256)S(1)}, s32[192]{0:T(256)}, u32[]{:S(2)}) copy-start(s32[192]{0:T(256)} %param.22) | copy-start | bytes 2308
  7.2 46.8 %collective-permute-start = (bf16[1024,16]{0,1:T(8,128)(2,1)}, bf16[1024,16]{0,1:T(8,128)(2,1)S(1)}, u32[]{:S(2)}, u32[]{:S(2)}) collective-permute-start(bf16[1024,16]{0,1:T(8,128)(2,1)} %param.14), channel_id=1, source_target_pairs={{0,120},{8,0},{16,8},{24,16},{32,24},{40,32},{48,40},{56,48},{64,5... | collective-permute-start | bytes 98312 | tf_op jit(solution)/shard_map/ppermute | solution.py:34
  18.7 45.6 %collective-permute-start.1 = (bf16[1024,16]{0,1:T(8,128)(2,1)}, bf16[1024,16]{0,1:T(8,128)(2,1)S(1)}, u32[]{:S(2)}, u32[]{:S(2)}) collective-permute-start(bf16[1024,16]{0,1:T(8,128)(2,1)} %param.14), channel_id=1, source_target_pairs={{0,112},{8,120},{16,0},{24,8},{32,16},{40,24},{48,32},{56,40},{64,... | collective-permute-start | bytes 98312 | tf_op jit(solution)/shard_map/ppermute | solution.py:34
  22.1 46.6 %collective-permute-start.2 = (bf16[1024,16]{0,1:T(8,128)(2,1)}, bf16[1024,16]{0,1:T(8,128)(2,1)S(1)}, u32[]{:S(2)}, u32[]{:S(2)}) collective-permute-start(bf16[1024,16]{0,1:T(8,128)(2,1)} %param.14), channel_id=1, source_target_pairs={{0,104},{8,112},{16,120},{24,0},{32,8},{40,16},{48,24},{56,32},{64... | collective-permute-start | bytes 98312 | tf_op jit(solution)/shard_map/ppermute | solution.py:34
  27.1 51.0 %collective-permute-start.3 = (bf16[1024,16]{0,1:T(8,128)(2,1)}, bf16[1024,16]{0,1:T(8,128)(2,1)S(1)}, u32[]{:S(2)}, u32[]{:S(2)}) collective-permute-start(bf16[1024,16]{0,1:T(8,128)(2,1)} %param.14), channel_id=1, source_target_pairs={{0,96},{8,104},{16,112},{24,120},{32,0},{40,8},{48,16},{56,24},{64... | collective-permute-start | bytes 98312 | tf_op jit(solution)/shard_map/ppermute | solution.py:34
  30.0 51.2 %collective-permute-start.4 = (bf16[1024,16]{0,1:T(8,128)(2,1)}, bf16[1024,16]{0,1:T(8,128)(2,1)S(1)}, u32[]{:S(2)}, u32[]{:S(2)}) collective-permute-start(bf16[1024,16]{0,1:T(8,128)(2,1)} %param.14), channel_id=1, source_target_pairs={{0,88},{8,96},{16,104},{24,112},{32,120},{40,0},{48,8},{56,16},{64... | collective-permute-start | bytes 98312 | tf_op jit(solution)/shard_map/ppermute | solution.py:34
  38.1 105.5 %all-to-all-start = ((bf16[64,3,1152]{2,1,0:T(4,128)(2,1)}), bf16[64,3,1152]{2,1,0:T(4,128)(2,1)S(1)}, u32[]{:S(2)}, u32[]{:S(2)}) async-start(bf16[64,3,1152]{2,1,0:T(4,128)(2,1)} %pad_maximum_fusion.1), calls=%async_computation.1 | async-start | bytes 1179648 | tf_op jit(solution)/shard_map/all_to_all | solution.py:91
  54.0 37.5 %collective-permute-start.5 = (bf16[1024,16]{0,1:T(8,128)(2,1)S(1)}, bf16[1024,16]{0,1:T(8,128)(2,1)S(1)}, u32[]{:S(2)}, u32[]{:S(2)}) collective-permute-start(bf16[1024,16]{0,1:T(8,128)(2,1)S(1)} %copy-done.7), channel_id=1, source_target_pairs={{0,80},{8,88},{16,96},{24,104},{32,112},{40,120},{48,0},{56,8},{64... | collective-permute-start | bytes 98312 | tf_op jit(solution)/shard_map/ppermute | solution.py:34
  64.4 33.8 %collective-permute-start.6 = (bf16[1024,16]{0,1:T(8,128)(2,1)S(1)}, bf16[1024,16]{0,1:T(8,128)(2,1)S(1)}, u32[]{:S(2)}, u32[]{:S(2)}) collective-permute-start(bf16[1024,16]{0,1:T(8,128)(2,1)S(1)} %copy-done.7), channel_id=1, source_target_pairs={{0,72},{8,80},{16,88},{24,96},{32,104},{40,112},{48,120},{56,0},{6... | collective-permute-start | bytes 98312 | tf_op jit(solution)/shard_map/ppermute | solution.py:34
  68.7 31.5 %collective-permute-start.7 = (bf16[1024,16]{0,1:T(8,128)(2,1)S(1)}, bf16[1024,16]{0,1:T(8,128)(2,1)S(1)}, u32[]{:S(2)}, u32[]{:S(2)}) collective-permute-start(bf16[1024,16]{0,1:T(8,128)(2,1)S(1)} %copy-done.7), channel_id=1, source_target_pairs={{0,64},{8,72},{16,80},{24,88},{32,96},{40,104},{48,112},{56,120},{... | collective-permute-start | bytes 98312 | tf_op jit(solution)/shard_map/ppermute | solution.py:34
  78.1 27.3 %collective-permute-start.8 = (bf16[1024,16]{0,1:T(8,128)(2,1)S(1)}, bf16[1024,16]{0,1:T(8,128)(2,1)S(1)}, u32[]{:S(2)}, u32[]{:S(2)}) collective-permute-start(bf16[1024,16]{0,1:T(8,128)(2,1)S(1)} %copy-done.7), channel_id=1, source_target_pairs={{0,56},{8,64},{16,72},{24,80},{32,88},{40,96},{48,104},{56,112},{6... | collective-permute-start | bytes 98312 | tf_op jit(solution)/shard_map/ppermute | solution.py:34
  81.2 26.9 %collective-permute-start.9 = (bf16[1024,16]{0,1:T(8,128)(2,1)S(1)}, bf16[1024,16]{0,1:T(8,128)(2,1)S(1)}, u32[]{:S(2)}, u32[]{:S(2)}) collective-permute-start(bf16[1024,16]{0,1:T(8,128)(2,1)S(1)} %copy-done.7), channel_id=1, source_target_pairs={{0,48},{8,56},{16,64},{24,72},{32,80},{40,88},{48,96},{56,104},{64... | collective-permute-start | bytes 98312 | tf_op jit(solution)/shard_map/ppermute | solution.py:34
  91.5 21.4 %collective-permute-start.10 = (bf16[1024,16]{0,1:T(8,128)(2,1)S(1)}, bf16[1024,16]{0,1:T(8,128)(2,1)S(1)}, u32[]{:S(2)}, u32[]{:S(2)}) collective-permute-start(bf16[1024,16]{0,1:T(8,128)(2,1)S(1)} %copy-done.7), channel_id=1, source_target_pairs={{0,40},{8,48},{16,56},{24,64},{32,72},{40,80},{48,88},{56,96},{64,... | collective-permute-start | bytes 98312 | tf_op jit(solution)/shard_map/ppermute | solution.py:34
  98.2 14.7 %collective-permute-start.11 = (bf16[1024,16]{0,1:T(8,128)(2,1)S(1)}, bf16[1024,16]{0,1:T(8,128)(2,1)S(1)}, u32[]{:S(2)}, u32[]{:S(2)}) collective-permute-start(bf16[1024,16]{0,1:T(8,128)(2,1)S(1)} %copy-done.7), channel_id=1, source_target_pairs={{0,32},{8,40},{16,48},{24,56},{32,64},{40,72},{48,80},{56,88},{64,... | collective-permute-start | bytes 98312 | tf_op jit(solution)/shard_map/ppermute | solution.py:34
  100.2 12.8 %collective-permute-start.12 = (bf16[1024,16]{0,1:T(8,128)(2,1)S(1)}, bf16[1024,16]{0,1:T(8,128)(2,1)S(1)}, u32[]{:S(2)}, u32[]{:S(2)}) collective-permute-start(bf16[1024,16]{0,1:T(8,128)(2,1)S(1)} %copy-done.7), channel_id=1, source_target_pairs={{0,24},{8,32},{16,40},{24,48},{32,56},{40,64},{48,72},{56,80},{64,... | collective-permute-start | bytes 98312 | tf_op jit(solution)/shard_map/ppermute | solution.py:34
  105.4 7.9 %collective-permute-start.13 = (bf16[1024,16]{0,1:T(8,128)(2,1)S(1)}, bf16[1024,16]{0,1:T(8,128)(2,1)S(1)}, u32[]{:S(2)}, u32[]{:S(2)}) collective-permute-start(bf16[1024,16]{0,1:T(8,128)(2,1)S(1)} %copy-done.7), channel_id=1, source_target_pairs={{0,16},{8,24},{16,32},{24,40},{32,48},{40,56},{48,64},{56,72},{64,... | collective-permute-start | bytes 98312 | tf_op jit(solution)/shard_map/ppermute | solution.py:34
  108.1 7.0 %collective-permute-start.14 = (bf16[1024,16]{0,1:T(8,128)(2,1)S(1)}, bf16[1024,16]{0,1:T(8,128)(2,1)S(1)}, u32[]{:S(2)}, u32[]{:S(2)}) collective-permute-start(bf16[1024,16]{0,1:T(8,128)(2,1)S(1)} %copy-done.7), channel_id=1, source_target_pairs={{0,8},{8,16},{16,24},{24,32},{32,40},{40,48},{48,56},{56,64},{64,7... | collective-permute-start | bytes 98312 | tf_op jit(solution)/shard_map/ppermute | solution.py:34
  115.4 22.0 %collective-permute-start.15 = (bf16[1024,256]{0,1:T(8,128)(2,1)S(1)}, bf16[1024,256]{0,1:T(8,128)(2,1)S(1)}, u32[]{:S(2)}, u32[]{:S(2)}) collective-permute-start(bf16[1024,256]{0,1:T(8,128)(2,1)S(1)} %bitcast.147), channel_id=1, source_target_pairs={{0,384},{128,0},{256,128},{384,256},{1,385},{129,1},{257,129},{385... | collective-permute-start | bytes 1572872 | tf_op jit(solution)/shard_map/ppermute | solution.py:34
  120.3 17.2 %collective-permute-start.16 = (bf16[1024,256]{0,1:T(8,128)(2,1)S(1)}, bf16[1024,256]{0,1:T(8,128)(2,1)S(1)}, u32[]{:S(2)}, u32[]{:S(2)}) collective-permute-start(bf16[1024,256]{0,1:T(8,128)(2,1)S(1)} %bitcast.148), channel_id=1, source_target_pairs={{0,256},{128,384},{256,0},{384,128},{1,257},{129,385},{257,1},{385... | collective-permute-start | bytes 1572872 | tf_op jit(solution)/shard_map/ppermute | solution.py:34
  123.9 0.8 copy-start.2
  124.6 18.5 %collective-permute-start.17 = (bf16[1024,256]{0,1:T(8,128)(2,1)S(1)}, bf16[1024,256]{0,1:T(8,128)(2,1)S(1)}, u32[]{:S(2)}, u32[]{:S(2)}) collective-permute-start(bf16[1024,256]{0,1:T(8,128)(2,1)S(1)} %bitcast.149), channel_id=1, source_target_pairs={{0,128},{128,256},{256,384},{384,0},{1,129},{129,257},{257,385},{3... | collective-permute-start | bytes 1572872 | tf_op jit(solution)/shard_map/ppermute | solution.py:34
  145.4 44.9 %all-to-all-start.1 = ((bf16[8,384,128]{1,2,0:T(8,128)(2,1)}), bf16[8,384,128]{1,2,0:T(8,128)(2,1)}, u32[]{:S(2)}, u32[]{:S(2)}) async-start(bf16[8,384,128]{1,2,0:T(8,128)(2,1)} %stack.89), calls=%async_computation.2 | async-start | bytes 1572864 | tf_op jit(solution)/shard_map/all_to_all | solution.py:83
  153.6 33.6 %copy-start.3 = (bf16[384,128]{1,0:T(8,128)(2,1)S(1)}, bf16[384,128]{1,0:T(8,128)(2,1)}, u32[]{:S(2)}) copy-start(bf16[384,128]{1,0:T(8,128)(2,1)} %copy-done.2) | copy-start | bytes 294916
  190.3 70.7 %all-to-all-start.2 = ((f32[3,64,1152]{2,0,1:T(4,128)}), f32[3,64,1152]{2,0,1:T(4,128)}, u32[]{:S(2)}, u32[]{:S(2)}) async-start(f32[3,64,1152]{2,0,1:T(4,128)} %copy.87), calls=%async_computation.3 | async-start | bytes 2359296 | tf_op jit(solution)/shard_map/all_to_all | solution.py:136
  200.9 43.2 %reduce-scatter.2.cloned.1.call-start = ((), (), s32[]{:S(2)}) async-start(), calls=%async_computation.4 | async-start | bytes 1769472 | tf_op jit(solution)/shard_map/reduce_scatter | solution.py:103
  208.5 56.4 %copy-start.4 = (bf16[128,1,16,64]{0,3,2,1:T(8,128)(2,1)S(1)}, bf16[128,1,16,64]{0,3,2,1:T(8,128)(2,1)}, u32[]{:S(2)}) copy-start(bf16[128,1,16,64]{0,3,2,1:T(8,128)(2,1)} %param.15) | copy-start | bytes 786436
  208.5 56.4 %copy-start.5 = (f32[128,1,16,64]{0,3,2,1:T(8,128)S(1)}, f32[128,1,16,64]{0,3,2,1:T(8,128)}, u32[]{:S(2)}) copy-start(f32[128,1,16,64]{0,3,2,1:T(8,128)} %param.16) | copy-start | bytes 1572868
  208.5 56.4 %copy-start.6 = (f32[128,1,16,64]{0,3,2,1:T(8,128)S(1)}, f32[128,1,16,64]{0,3,2,1:T(8,128)}, u32[]{:S(2)}) copy-start(f32[128,1,16,64]{0,3,2,1:T(8,128)} %param.17) | copy-start | bytes 1572868
  260.9 5.4 %copy-start.1 = (bf16[128,1,128]{2,0,1:T(8,128)(2,1)S(1)}, bf16[128,1,128]{2,0,1:T(8,128)(2,1)}, u32[]{:S(2)}) copy-start(bf16[128,1,128]{2,0,1:T(8,128)(2,1)} %param.18) | copy-start | bytes 98308
  260.9 5.4 %copy-start.8 = (f32[128,1,128]{2,1,0:T(1,128)S(1)}, f32[128,1,128]{2,1,0:T(1,128)}, u32[]{:S(2)}) copy-start(f32[128,1,128]{2,1,0:T(1,128)} %param.19) | copy-start | bytes 196612
  260.9 5.4 %copy-start.9 = (f32[128,1,128]{2,1,0:T(1,128)S(1)}, f32[128,1,128]{2,1,0:T(1,128)}, u32[]{:S(2)}) copy-start(f32[128,1,128]{2,1,0:T(1,128)} %param.20) | copy-start | bytes 196612
Sparse Core Ops, SparseCore 0:
  204.5 39.4 reduce-scatter.1
